TPU v7x, 128 devices: a whole 4x4x4 slice. The times are simulated.
128 devices in a mesh: item: 4 (over y_hi, core), row: 8 (over y_lo, x), col: 4 (over z).
Axes of the slice: x: 4, y: 4 (y_hi: 2, y_lo: 2; y = y_hi * 2 + y_lo), z: 4, core: 2. Of those that a mesh axis runs over, the one named last changes fastest.
Arguments:
- latents: bfloat16 [64, 64, 4, 2432], P('row', 'col', 'item'), may hold values from -6 to 6
- prompt_tokens: bfloat16 [160, 4, 2432], P('row', 'item'), may hold values from -6 to 6
- text_count: int32 [4], P('item'), may hold values from 1 to 160, as said below
- step_index: int32 [4], P('item'), may hold values from 0 to 27
- step_table: float32 [28, 6, 2432], replicated, may hold values from -3 to 3
- item_mod: float32 [4, 6, 2432], P('item'), may hold values from -3 to 3
- w_qkv: bfloat16 [2432, 3, 1536], P(None, None, 'col'), may hold values from -1 to 1
- w_kv_text: bfloat16 [2432, 2, 1536], P(None, None, 'col'), may hold values from -0.125 to 0.125
- q_gain: float32 [64], replicated, may hold values from 0.5 to 6.5
- k_gain: float32 [64], replicated, may hold values from 0.5 to 6.5
- w_out: bfloat16 [1536, 2432], P('col'), may hold values from -0.15625 to 0.15625
- w_up: bfloat16 [2432, 9728], P(None, ('item', 'col')), may hold values from -0.125 to 0.125
- w_down: bfloat16 [9728, 2432], P(('item', 'col')), may hold values from -0.0625 to 0.0625
Outputs:
- updated: bfloat16 [64, 64, 4, 2432], P('row', 'col', 'item')
Inputs may be any that keep to these rules, and one draw needn't show every extreme that they name: `text_count`: some item has all 160 text tokens live.
All inputs are finite; a program needn't handle non-finite values.
Results may differ from a plain program's by a relative error of at most 0.022.
The roundings to bfloat16 on the way count: a program that leaves them out, or rounds other values in their place, can miss the bound.
Values may be sent and summed in bfloat16 or wider, within the bound.
No kernel may reach another device: no remote copies, remote signals or barrier semaphores. Data moves between devices by JAX's collectives and lax.ppermute only.
A program may use at most 192 MiB of HBM per device.

v0:
```python
import jax
import jax.numpy as jnp
from jax import lax
from jax.sharding import PartitionSpec as P

epsilon = 1e-06


def layer_norm(values):
    values = values.astype(jnp.float32)
    center = values - jnp.mean(values, axis=-1, keepdims=True)
    variance = jnp.mean(center * center, axis=-1, keepdims=True)
    return center * lax.rsqrt(variance + epsilon)


def rms_heads(values, gain):
    return values * lax.rsqrt(jnp.mean(values * values, axis=-1, keepdims=True) + epsilon) * gain


def local(
    latents,
    prompt_tokens,
    text_count,
    step_index,
    step_table,
    item_mod,
    w_qkv,
    w_kv_text,
    q_gain,
    k_gain,
    w_out,
    w_up,
    w_down,
):
    grid_rows, grid_cols, local_items, model_width = latents.shape
    own_rows = grid_rows * grid_cols
    tokens = latents.reshape(own_rows, local_items, model_width)
    wide_up, wide_down = (w_up, w_down)
    chosen = (
        step_index[:, None] == jnp.arange(step_table.shape[0], dtype=jnp.int32)[None, :]
    ).astype(jnp.float32)
    modulation = (
        jnp.einsum("is,sjd->ijd", chosen, step_table, precision=lax.Precision.HIGHEST) + item_mod
    )
    strip_rows = lax.all_gather(tokens, "col", axis=0, tiled=True)
    strip_len = strip_rows.shape[0]
    normed_one = (layer_norm(strip_rows) * (1.0 + modulation[:, 1]) + modulation[:, 0]).astype(
        jnp.bfloat16
    )
    projected = jnp.einsum("sid,dce->csie", normed_one, w_qkv, preferred_element_type=jnp.float32)
    head_cols = w_qkv.shape[2]
    local_heads = head_cols // 64
    query = rms_heads(projected[0].reshape(strip_len, local_items, local_heads, 64), q_gain).astype(
        jnp.bfloat16
    )
    key_img = (
        rms_heads(projected[1].reshape(strip_len, local_items, local_heads, 64), k_gain)
        .astype(jnp.bfloat16)
        .reshape(strip_len, local_items, head_cols)
    )
    value_img = projected[2].astype(jnp.bfloat16)
    text_len = prompt_tokens.shape[0]
    text_normed = layer_norm(prompt_tokens).astype(jnp.bfloat16)
    text_proj = jnp.einsum(
        "tid,dce->ctie", text_normed, w_kv_text, preferred_element_type=jnp.float32
    )
    text_key = (
        rms_heads(text_proj[0].reshape(text_len, local_items, local_heads, 64), k_gain)
        .astype(jnp.bfloat16)
        .reshape(text_len, local_items, head_cols)
    )
    text_value = text_proj[1].astype(jnp.bfloat16)
    position = lax.axis_index("row") * text_len + jnp.arange(text_len, dtype=jnp.int32)
    text_bias = jnp.where(position[:, None] < text_count[None, :], 0.0, -jnp.inf).astype(
        jnp.float32
    )
    run_max = jnp.full((local_items, local_heads, strip_len), -jnp.inf, jnp.float32)
    run_sum = jnp.zeros((local_items, local_heads, strip_len), jnp.float32)
    accum = jnp.zeros((local_items, local_heads, strip_len, 64), jnp.float32)
    key_piece = lax.all_gather(key_img, "row", axis=0, tiled=True)
    value_piece = lax.all_gather(value_img, "row", axis=0, tiled=True)
    tkey_piece = lax.all_gather(text_key, "row", axis=0, tiled=True)
    tvalue_piece = lax.all_gather(text_value, "row", axis=0, tiled=True)
    bias_piece = lax.all_gather(text_bias.astype(jnp.bfloat16), "row", axis=0, tiled=True).astype(
        jnp.float32
    )
    key_piece = key_piece.reshape(key_piece.shape[0], local_items, local_heads, 64)
    value_piece = value_piece.reshape(value_piece.shape[0], local_items, local_heads, 64)
    tkey_piece = tkey_piece.reshape(tkey_piece.shape[0], local_items, local_heads, 64)
    tvalue_piece = tvalue_piece.reshape(tvalue_piece.shape[0], local_items, local_heads, 64)
    score_img = (
        jnp.einsum("sihd,kihd->ihsk", query, key_piece, preferred_element_type=jnp.float32) * 0.125
    )
    score_txt = (
        jnp.einsum("sihd,kihd->ihsk", query, tkey_piece, preferred_element_type=jnp.float32) * 0.125
    )
    score_txt = score_txt + jnp.transpose(bias_piece)[:, None, None, :]
    new_max = jnp.maximum(
        run_max, jnp.maximum(jnp.max(score_img, axis=-1), jnp.max(score_txt, axis=-1))
    )
    rescale = jnp.exp(run_max - new_max)
    prob_img = jnp.exp(score_img - new_max[..., None])
    prob_txt = jnp.exp(score_txt - new_max[..., None])
    run_sum = run_sum * rescale + jnp.sum(prob_img, axis=-1) + jnp.sum(prob_txt, axis=-1)
    accum = accum * rescale[..., None]
    accum = accum + jnp.einsum(
        "ihsk,kihd->ihsd",
        prob_img.astype(jnp.bfloat16),
        value_piece,
        preferred_element_type=jnp.float32,
    )
    accum = accum + jnp.einsum(
        "ihsk,kihd->ihsd",
        prob_txt.astype(jnp.bfloat16),
        tvalue_piece,
        preferred_element_type=jnp.float32,
    )
    run_max, run_sum, accum = (new_max, run_sum, accum)
    heads_out = (accum / run_sum[..., None]).astype(jnp.bfloat16)
    attended = jnp.transpose(heads_out, (2, 0, 1, 3)).reshape(strip_len, local_items, head_cols)
    block_rows = attended
    attn_out = lax.psum_scatter(
        jnp.einsum("sie,ed->sid", block_rows, w_out, preferred_element_type=jnp.float32).astype(
            jnp.bfloat16
        ),
        "col",
        scatter_dimension=0,
        tiled=True,
    ).astype(jnp.float32)
    residual = (tokens.astype(jnp.float32) + modulation[:, 2] * attn_out).astype(jnp.bfloat16)
    normed_two = (layer_norm(residual) * (1.0 + modulation[:, 4]) + modulation[:, 3]).astype(
        jnp.bfloat16
    )
    residual, flat_rows = (residual, normed_two.reshape(own_rows * local_items, model_width))
    hidden = jax.nn.gelu(
        jnp.dot(
            lax.all_gather(flat_rows, ("item", "col"), axis=0, tiled=True),
            wide_up,
            preferred_element_type=jnp.float32,
        ),
        approximate=True,
    ).astype(jnp.bfloat16)
    block_rows = hidden
    mlp_sum = lax.psum_scatter(
        jnp.dot(block_rows, wide_down, preferred_element_type=jnp.float32).astype(jnp.bfloat16),
        ("item", "col"),
        scatter_dimension=0,
        tiled=True,
    ).astype(jnp.float32)
    mlp_sum = mlp_sum.reshape(own_rows, local_items, model_width)
    updated = (residual.astype(jnp.float32) + modulation[:, 5] * mlp_sum).astype(jnp.bfloat16)
    return updated.reshape(grid_rows, grid_cols, local_items, model_width)


def solution(mesh):
    placed = (
        P("row", "col", "item", None),
        P("row", "item", None),
        P("item"),
        P("item"),
        P(),
        P("item", None, None),
        P(None, None, "col"),
        P(None, None, "col"),
        P(),
        P(),
        P("col", None),
        P(None, ("item", "col")),
        P(("item", "col"), None),
    )
    return jax.shard_map(
        local, mesh=mesh, in_specs=placed, out_specs=P("row", "col", "item", None), check_vma=False
    )
```

profile of v0, /device:TPU:1, one launch (start us, length us, event | category | flops | bytes accessed | tf_op | source)
XLA Modules:
  0.0 471.7 jit_solution(10957942517682658492)
XLA Ops:
  8.1 2.2 fusion.77
  11.1 0.9 reshape_add_fusion
  12.1 34.5 %all-gather.8.cloned.1.call-done = bf16[512,1,2432]{2,0,1:T(8,128)(2,1)} async-done(((bf16[128,1,2432]{2,0,1:T(8,128)(2,1)}), bf16[512,1,2432]{2,0,1:T(8,128)(2,1)}) %all-gather.8.cloned.1.call-update) | async-done | bytes 2490384 | tf_op jit(solution)/shard_map/all_gather | solution.py:45
  46.6 2.3 convert_reduce_fusion
  49.0 0.8 fusion.8
  49.8 6.1 %fusion.39 = f32[3,512,1,384]{1,3,0,2:T(8,128)S(1)} fusion(bf16[2432,3,384]{2,0,1:T(8,128)(2,1)} %param.19, bf16[512,1,2432]{2,0,1:T(8,128)(2,1)S(1)} %copy-done.1, f32[2432]{0:T(1024)S(1)} %get-tuple-element.8, f32[2432]{0:T(1024)S(1)} %get-tuple-element.9, f32[512]{0:T(512)S(1)} %add_rsqrt_fusion.3, f32[512]{0:T(512)S(1)} %broadcast_multiply_fusion), kind=kOutput, calls=%fused_computation.45 | convolution fusion | flops 2876375040 | bytes 10476544 | tf_op jit(solution)/shard_map/sid,dce->csie/dot_general | solution.py:50
  56.0 1.4 copy-done.4
  57.4 1.6 slice_multiply_fusion.2
  59.0 1.2 reduce_sum.102
  60.3 2.1 fusion.64
  62.9 2.7 fusion.56
  66.0 25.3 %all_gather.23 = bf16[160,1,384]{2,1,0:T(2,128)(2,1)S(1)} all-gather(bf16[20,1,384]{2,1,0:T(2,128)(2,1)S(1)} %copy.26), channel_id=1, replica_groups=mesh['item'=4,'row'=8,'col'=4] {'row'}, dimensions={0}, use_global_device_ids=true | all-gather | bytes 138240 | tf_op jit(solution)/shard_map/all_gather | solution.py:82
  93.6 16.2 %all-reduce = bf16[160]{0:T(256)(128)(2,1)S(1)} all-reduce(bf16[160]{0:T(256)(128)(2,1)S(1)} %dynamic-update-slice), channel_id=1, replica_groups=mesh['item'=4,'row'=8,'col'=4] {'row'}, use_global_device_ids=true, to_apply=%add | all-reduce | flops 160 | bytes 640
  109.8 22.0 %all-gather.1 = bf16[1,160,1,384]{3,2,0,1:T(2,128)(2,1)S(1)} all-gather(bf16[1,20,1,384]{3,2,0,1:T(2,128)(2,1)S(1)} %copy.28), channel_id=3, replica_groups=mesh['item'=4,'row'=8,'col'=4] {'row'}, dimensions={1}, use_global_device_ids=true | all-gather | bytes 138240 | tf_op jit(solution)/shard_map/all_gather | solution.py:83
  131.8 0.9 copy.29
  132.7 1.9 slice.74
  134.7 1.2 reduce_sum.101
  136.2 2.9 fusion.38
  139.1 21.7 %multiply_reduce_fusion = (f32[6,512]{1,0:T(8,128)S(1)}, f32[6,512,4096]{2,1,0:T(8,128)}) fusion(bf16[4096,6,64]{0,2,1:T(8,128)(2,1)} %bitcast.91, f32[512,6,64]{0,2,1:T(8,128)} %bitcast.90, f32[64]{0:T(128)S(1)} %copy-done.8, f32[512,6]{0,1:T(8,128)S(1)} %add_rsqrt_fusion.1), kind=kOutput, calls=%fused_computation.1 | convolution fusion | flops 1636365312 | bytes 54288640 | tf_op jit(solution)/shard_map/sihd,kihd->ihsk/dot_general | solution.py:92
  160.7 2.1 fusion.42
  162.8 20.8 %fusion = f32[6,512]{1,0:T(8,128)S(1)} fusion(f32[6,512,4096]{2,1,0:T(8,128)} %get-tuple-element.19, f32[6,512]{1,0:T(8,128)S(1)} %get-tuple-element.14), kind=kLoop, calls=%fused_computation.2 | loop fusion | flops 37745664 | bytes 50356224 | tf_op jit(solution)/shard_map/reduce_sum | solution.py:104
  183.6 4.3 all-gather.12.cloned.1.call-done
  187.9 19.8 %fusion.47 = f32[6,512,64]{1,2,0:T(8,128)S(1)} fusion(bf16[4096,6,64]{0,2,1:T(8,128)(2,1)} %bitcast.95, f32[6,512,4096]{2,1,0:T(8,128)} %get-tuple-element.19, f32[6,512]{1,0:T(8,128)S(1)} %get-tuple-element.14, f32[6,512]{1,0:T(8,128)S(1)} %get-tuple-element.13), kind=kOutput, calls=%fused_computation.52 | convolution fusion | flops 1648558080 | bytes 54288384 | tf_op jit(solution)/shard_map/ihsk,kihd->ihsd/dot_general | solution.py:106
  208.4 0.8 copy-done.5
  209.2 3.0 fusion.20
  212.3 39.9 %reduce-scatter.3.cloned.1.call-done = bf16[128,1,2432]{2,0,1:T(8,128)(2,1)} async-done(((bf16[512,1,2432]{2,0,1:T(8,128)(2,1)}), bf16[128,1,2432]{2,0,1:T(8,128)(2,1)}) %reduce-scatter.3.cloned.1.call-update) | async-done | bytes 622608 | tf_op jit(solution)/shard_map/reduce_scatter | solution.py:122
  252.2 1.6 convert_reduce_fusion.1
  254.6 1.3 fusion.54
  256.2 79.7 %all-gather.14.cloned.1.call-done = bf16[2048,1,2432]{2,0,1:T(8,128)(2,1)} async-done(((bf16[128,1,2432]{2,0,1:T(8,128)(2,1)}), bf16[2048,1,2432]{2,0,1:T(8,128)(2,1)}) %all-gather.14.cloned.1.call-update) | async-done | bytes 9961488 | tf_op jit(solution)/shard_map/all_gather | solution.py:137
  335.8 20.5 %convolution_convert_fusion = bf16[2048,2432]{1,0:T(8,128)(2,1)} fusion(bf16[608,2432]{1,0:T(8,128)(2,1)S(1)} %copy-done, bf16[2432,608]{0,1:T(8,128)(2,1)} %param.24, bf16[2048,1,2432]{2,0,1:T(8,128)(2,1)} %all-gather.14.cloned.1.call-done), kind=kOutput, calls=%fused_computation.5 | convolution fusion | flops 12129337344 | bytes 25837568 | tf_op jit(solution)/shard_map/dot_general | solution.py:145
  356.3 106.2 %reduce-scatter.5.cloned.1.call-done = bf16[128,2432]{1,0:T(8,128)(2,1)} async-done(((bf16[2048,2432]{1,0:T(8,128)(2,1)}), bf16[128,2432]{1,0:T(8,128)(2,1)}) %reduce-scatter.5.cloned.1.call-update) | async-done | bytes 622608 | tf_op jit(solution)/shard_map/reduce_scatter | solution.py:144
  462.6 2.3 fusion.55
  (66 shorter events, 5.9 us)
Async XLA Ops:
  6.5 329.3 %copy-start = (bf16[608,2432]{1,0:T(8,128)(2,1)S(1)}, bf16[608,2432]{1,0:T(8,128)(2,1)}, u32[]{:S(2)}) copy-start(bf16[608,2432]{1,0:T(8,128)(2,1)} %param.25) | copy-start | bytes 8871940
  6.5 40.1 %all-gather.8.cloned.1.call-start = ((), (), s32[]{:S(2)}) async-start(), calls=%async_computation.2 | async-start | bytes 3112960 | tf_op jit(solution)/shard_map/all_gather | solution.py:45
  7.3 131.8 %all-gather.10.cloned.1.call-start = ((), (), s32[]{:S(2)}) async-start(), calls=%async_computation.3 | async-start | bytes 3538944 | tf_op jit(solution)/shard_map/all_gather | solution.py:80
  46.6 2.5 copy-start.1
  56.0 1.4 copy-start.4
  59.0 3.5 copy-start.6
  62.4 29.8 %copy-start.9 = (u32[128]{0:T(128)S(1)}, u32[128]{0:T(128)}, u32[]{:S(2)}) copy-start(u32[128]{0:T(128)} %constant.56) | copy-start | bytes 1540
  62.4 125.4 %all-gather.12.cloned.1.call-start = ((), (), s32[]{:S(2)}) async-start(), calls=%async_computation.6 | async-start | bytes 3538944 | tf_op jit(solution)/shard_map/all_gather | solution.py:81
  65.6 70.6 %copy-start.8 = (f32[64]{0:T(128)S(1)}, f32[64]{0:T(128)}, u32[]{:S(2)}) copy-start(f32[64]{0:T(128)} %param.21) | copy-start | bytes 772
  135.9 116.3 %reduce-scatter.3.cloned.1.call-start = ((), (), s32[]{:S(2)}) async-start(), calls=%async_computation.4 | async-start | bytes 3112960 | tf_op jit(solution)/shard_map/reduce_scatter | solution.py:122
  187.8 19.9 %copy-start.3 = (f32[6,512,160]{1,2,0:T(8,128)S(1)}, f32[6,512,160]{1,2,0:T(8,128)}, u32[]{:S(2)}) copy-start(f32[6,512,160]{1,2,0:T(8,128)} %get-tuple-element.21) | copy-start | bytes 5898244
  187.8 19.9 %copy-start.7 = (bf16[1,160,1,384]{1,3,2,0:T(8,128)(2,1)S(1)}, bf16[1,160,1,384]{1,3,2,0:T(8,128)(2,1)}, u32[]{:S(2)}) copy-start(bf16[1,160,1,384]{1,3,2,0:T(8,128)(2,1)} %copy.29) | copy-start | bytes 368644
  207.7 1.5 copy-start.5
  212.2 123.6 %all-gather.14.cloned.1.call-start = ((), (), s32[]{:S(2)}) async-start(), calls=%async_computation.7 | async-start | bytes 10584064 | tf_op jit(solution)/shard_map/all_gather | solution.py:137
  253.7 0.8 copy-start.2
  255.9 206.7 %reduce-scatter.5.cloned.1.call-start = ((), (), s32[]{:S(2)}) async-start(), calls=%async_computation.5 | async-start | bytes 10584064 | tf_op jit(solution)/shard_map/reduce_scatter | solution.py:144
Sparse Core Ops, SparseCore 0:
  9.0 37.5 all-gather.7
  62.5 44.3 all-gather.9
  136.0 51.7 all-gather.11
  212.3 39.7 reduce-scatter.2
  256.0 79.7 all-gather.13
  356.5 106.0 reduce-scatter.4
where the time goes:
time: 473 us; the launch traced here: 472 us
  waiting for transfers between devices  265 us (56%)
  matrix products  79.6 us (17%)
  blocking collectives  63.5 us (13%)
  other arithmetic  39 us (8%)
  between operations  15.7 us (3%)
  local copies, waits for them, and re-layouts  7.92 us (2%)
    reduce_scatter x1, waiting for transfers between devices, local(): lax.psum_scatter(jnp.dot(block_rows, wide_down, preferred_element_type=jn...  106 us
    all_gather x1, waiting for transfers between devices, local(): lax.all_gather(flat_rows, ('item', 'col'), axis=0, tiled=True)  79.7 us
    reduce_scatter x1, waiting for transfers between devices, local(): lax.psum_scatter(jnp.einsum('sie,ed->sid', block_rows, w_out, preferred_e...  39.9 us
    all_gather x1, waiting for transfers between devices, local(): strip_rows = lax.all_gather(tokens, 'col', axis=0, tiled=True)  34.5 us
    all_gather x1, blocking collectives, local(): tkey_piece = lax.all_gather(text_key, 'row', axis=0, tiled=True)  25.3 us
    all_gather x1, blocking collectives, local(): tvalue_piece = lax.all_gather(text_value, 'row', axis=0, tiled=True)  22 us
    dot_general x1, matrix products, local(): jnp.einsum('sihd,kihd->ihsk', query, key_piece, preferred_element_type=jn...  21.7 us
    reduce_sum x1, other arithmetic, local(): jnp.sum(prob_img, axis=-1)  20.8 us
  transfers between devices with their start and end apart: 6, of which 5 were waited for; matrix products, arithmetic and copies ran while one was open for 13% of the time, Pallas kernels for 0%

commit v1 on v0

v1 whole, which is shorter than its diff:
```python
import jax
import jax.numpy as jnp
from jax import lax
from jax.sharding import Mesh
from jax.sharding import PartitionSpec as P

epsilon = 1e-06
ITEM = ("ih", "ic")


def layer_norm(values):
    values = values.astype(jnp.float32)
    center = values - jnp.mean(values, axis=-1, keepdims=True)
    variance = jnp.mean(center * center, axis=-1, keepdims=True)
    return center * lax.rsqrt(variance + epsilon)


def rms_heads(values, gain):
    return values * lax.rsqrt(jnp.mean(values * values, axis=-1, keepdims=True) + epsilon) * gain


def local(
    latents,
    prompt_tokens,
    text_count,
    step_index,
    step_table,
    item_mod,
    w_qkv,
    w_kv_text,
    q_gain,
    k_gain,
    w_out,
    w_up,
    w_down,
):
    swap = [(0, 1), (1, 0)]
    other_up = lax.ppermute(w_up, "ic", swap)
    other_down = lax.ppermute(w_down, "ic", swap)

    grid_rows, grid_cols, local_items, model_width = latents.shape
    own_rows = grid_rows * grid_cols
    tokens = latents.reshape(own_rows, local_items, model_width)
    chosen = (
        step_index[:, None] == jnp.arange(step_table.shape[0], dtype=jnp.int32)[None, :]
    ).astype(jnp.float32)
    modulation = (
        jnp.einsum("is,sjd->ijd", chosen, step_table, precision=lax.Precision.HIGHEST) + item_mod
    )
    strip_rows = lax.all_gather(tokens, "col", axis=0, tiled=True)
    strip_len = strip_rows.shape[0]
    normed_one = (layer_norm(strip_rows) * (1.0 + modulation[:, 1]) + modulation[:, 0]).astype(
        jnp.bfloat16
    )
    projected = jnp.einsum("sid,dce->csie", normed_one, w_qkv, preferred_element_type=jnp.float32)
    head_cols = w_qkv.shape[2]
    local_heads = head_cols // 64
    query = rms_heads(projected[0].reshape(strip_len, local_items, local_heads, 64), q_gain).astype(
        jnp.bfloat16
    )
    key_img = (
        rms_heads(projected[1].reshape(strip_len, local_items, local_heads, 64), k_gain)
        .astype(jnp.bfloat16)
        .reshape(strip_len, local_items, head_cols)
    )
    value_img = projected[2].astype(jnp.bfloat16)
    text_len = prompt_tokens.shape[0]
    text_normed = layer_norm(prompt_tokens).astype(jnp.bfloat16)
    text_proj = jnp.einsum(
        "tid,dce->ctie", text_normed, w_kv_text, preferred_element_type=jnp.float32
    )
    text_key = (
        rms_heads(text_proj[0].reshape(text_len, local_items, local_heads, 64), k_gain)
        .astype(jnp.bfloat16)
        .reshape(text_len, local_items, head_cols)
    )
    text_value = text_proj[1].astype(jnp.bfloat16)

    piece_len = strip_len + text_len
    kv_local = jnp.stack(
        [
            jnp.concatenate([key_img, text_key], axis=0),
            jnp.concatenate([value_img, text_value], axis=0),
        ],
        axis=1,
    )
    kv_all = lax.all_gather(kv_local, "row", axis=0, tiled=True)
    n_keys = kv_all.shape[0]
    kv_all = kv_all.reshape(n_keys, 2, local_items, local_heads, 64)
    key_all = kv_all[:, 0]
    value_all = kv_all[:, 1]

    slot = jnp.arange(n_keys, dtype=jnp.int32)
    within = slot % piece_len
    text_pos = (slot // piece_len) * text_len + (within - strip_len)
    live = (within < strip_len)[:, None] | (text_pos[:, None] < text_count[None, :])
    bias = jnp.where(live, 0.0, -jnp.inf).astype(jnp.float32)

    scores = (
        jnp.einsum("sihd,kihd->ihsk", query, key_all, preferred_element_type=jnp.float32) * 0.125
    )
    scores = scores + jnp.transpose(bias)[:, None, None, :]
    row_max = jnp.max(scores, axis=-1, keepdims=True)
    probs = jnp.exp(scores - row_max)
    denom = jnp.sum(probs, axis=-1)
    accum = jnp.einsum(
        "ihsk,kihd->ihsd",
        probs.astype(jnp.bfloat16),
        value_all,
        preferred_element_type=jnp.float32,
    )
    heads_out = (accum / denom[..., None]).astype(jnp.bfloat16)
    attended = jnp.transpose(heads_out, (2, 0, 1, 3)).reshape(strip_len, local_items, head_cols)
    attn_out = lax.psum_scatter(
        jnp.einsum("sie,ed->sid", attended, w_out, preferred_element_type=jnp.float32).astype(
            jnp.bfloat16
        ),
        "col",
        scatter_dimension=0,
        tiled=True,
    ).astype(jnp.float32)
    residual = (tokens.astype(jnp.float32) + modulation[:, 2] * attn_out).astype(jnp.bfloat16)
    normed_two = (layer_norm(residual) * (1.0 + modulation[:, 4]) + modulation[:, 3]).astype(
        jnp.bfloat16
    )
    flat_rows = normed_two.reshape(own_rows * local_items, model_width)

    gathered = lax.all_gather(flat_rows, ("ih", "col"), axis=0, tiled=True)

    def half(up, down):
        hidden = jax.nn.gelu(
            jnp.dot(gathered, up, preferred_element_type=jnp.float32), approximate=True
        ).astype(jnp.bfloat16)
        return jnp.dot(hidden, down, preferred_element_type=jnp.float32)

    partial = half(w_up, w_down) + half(other_up, other_down)
    mlp_sum = lax.psum_scatter(
        partial.astype(jnp.bfloat16),
        ("ih", "col"),
        scatter_dimension=0,
        tiled=True,
    ).astype(jnp.float32)
    mlp_sum = mlp_sum.reshape(own_rows, local_items, model_width)
    updated = (residual.astype(jnp.float32) + modulation[:, 5] * mlp_sum).astype(jnp.bfloat16)
    return updated.reshape(grid_rows, grid_cols, local_items, model_width)


def solution(mesh):
    n_item = mesh.shape["item"]
    devices = mesh.devices.reshape(
        (n_item // 2, 2, mesh.shape["row"], mesh.shape["col"])
    )
    split_mesh = Mesh(devices, ("ih", "ic", "row", "col"))
    placed = (
        P("row", "col", ITEM, None),
        P("row", ITEM, None),
        P(ITEM),
        P(ITEM),
        P(),
        P(ITEM, None, None),
        P(None, None, "col"),
        P(None, None, "col"),
        P(),
        P(),
        P("col", None),
        P(None, (ITEM + ("col",))),
        P((ITEM + ("col",)), None),
    )
    return jax.shard_map(
        local,
        mesh=split_mesh,
        in_specs=placed,
        out_specs=P("row", "col", ITEM, None),
        check_vma=False,
    )
```

time: 473 us -> 455 us (0.962)
  blocking collectives: 63.5 us -> 0 us
  waiting for transfers between devices: 265 us -> 298 us
  local copies, waits for them, and re-layouts: 7.92 us -> 23.7 us
  other arithmetic: 39 us -> 30.9 us
  matrix products: 79.6 us -> 85.5 us
    all_gather x3 -> x2, waiting for transfers between devices: 83.9 us -> 149 us  [the longest x1 76.3 us: local(): gathered = lax.all_gather(flat_rows, ('ih', 'col'), axis=0, tiled=True)]
    all_gather x2 -> x0, blocking collectives: 47.3 us -> none  [the longest x1 25.3 us: local(): tkey_piece = lax.all_gather(text_key, 'row', axis=0, tiled=True)]
    reduce_scatter x2, waiting for transfers between devices: 146 us -> 119 us  [the longest x1 87.1 us: local(): lax.psum_scatter(partial.astype(jnp.bfloat16), ('ih', 'col'), scatter_dim...]
    all_gather x2 -> x1, local copies, waits for them, and re-layouts: 1.1 us -> 17.9 us  [local(): kv_all = lax.all_gather(kv_local, 'row', axis=0, tiled=True)]
    unnamed x1 -> x0, blocking collectives: 16.2 us -> none
    reduce_sum x2 -> x1, other arithmetic: 22.8 us -> 17.1 us  [local(): denom = jnp.sum(probs, axis=-1)]
    all_gather x1, waiting for transfers between devices: 34.5 us -> 29.3 us  [local(): strip_rows = lax.all_gather(tokens, 'col', axis=0, tiled=True)]
    dot_general x6 -> x5, matrix products: 68.5 us -> 73.5 us  [the longest x2 28.2 us: half(): return jnp.dot(hidden, down, preferred_element_type=jnp.float32)]
  transfers between devices with their start and end apart: 6 -> 7, of which waited for: 5 -> 5; matrix products, arithmetic and copies ran while one was open for 13% -> 5% of each run, Pallas kernels for 0% -> 0%
where the time goes in v1:
time: 455 us; the launch traced here: 454 us
  waiting for transfers between devices  298 us (65%)
  matrix products  85.5 us (19%)
  other arithmetic  30.9 us (7%)
  local copies, waits for them, and re-layouts  23.7 us (5%)
  between operations  14.7 us (3%)
    reduce_scatter x1, waiting for transfers between devices, local(): lax.psum_scatter(partial.astype(jnp.bfloat16), ('ih', 'col'), scatter_dim...  87.1 us
    all_gather x1, waiting for transfers between devices, local(): gathered = lax.all_gather(flat_rows, ('ih', 'col'), axis=0, tiled=True)  76.3 us
    all_gather x1, waiting for transfers between devices, local(): kv_all = lax.all_gather(kv_local, 'row', axis=0, tiled=True)  72.3 us
    reduce_scatter x1, waiting for transfers between devices, local(): lax.psum_scatter(jnp.einsum('sie,ed->sid', attended, w_out, preferred_ele...  32.1 us
    all_gather x1, waiting for transfers between devices, local(): strip_rows = lax.all_gather(tokens, 'col', axis=0, tiled=True)  29.3 us
    dot_general x2, matrix products, half(): return jnp.dot(hidden, down, preferred_element_type=jnp.float32)  28.2 us
    dot_general x1, matrix products, local(): jnp.einsum('ihsk,kihd->ihsd', probs.astype(jnp.bfloat16), value_all, pref...  21.3 us
    dot_general x1, matrix products, local(): jnp.einsum('sihd,kihd->ihsk', query, key_all, preferred_element_type=jnp....  20.9 us
  transfers between devices with their start and end apart: 7, of which 5 were waited for; matrix products, arithmetic and copies ran while one was open for 5% of the time, Pallas kernels for 0%

profile of v1, /device:TPU:1, one launch (start us, length us, event | category | flops | bytes accessed | tf_op | source)
XLA Modules:
  0.0 454.0 jit_solution(16406768502674731294)
XLA Ops:
  6.5 0.7 all-gather.5.cloned.1.call-update
  7.9 2.2 fusion.96
  10.2 0.7 mul.289
  10.9 1.0 convert_reduce_fusion.2
  12.0 1.1 fusion.74
  13.1 3.7 fusion.53
  17.3 29.3 %all-gather.5.cloned.1.call-done = bf16[512,1,2432]{2,0,1:T(8,128)(2,1)} async-done(((bf16[128,1,2432]{2,0,1:T(8,128)(2,1)}), bf16[512,1,2432]{2,0,1:T(8,128)(2,1)}) %all-gather.5.cloned.1.call-update) | async-done | bytes 2490384 | tf_op jit(solution)/shard_map/all_gather | solution.py:50
  46.6 2.3 convert_reduce_fusion
  49.0 0.8 fusion.7
  49.8 6.1 %fusion.36 = f32[512,3,384]{0,2,1:T(8,128)S(1)} fusion(bf16[2432,3,384]{2,0,1:T(8,128)(2,1)} %param.19, bf16[512,1,2432]{2,0,1:T(8,128)(2,1)S(1)} %copy-done.1, f32[2432]{0:T(1024)S(1)} %get-tuple-element.8, f32[2432]{0:T(1024)S(1)} %get-tuple-element.9, f32[512]{0:T(512)S(1)} %add_rsqrt_fusion.3, f32[512]{0:T(512)S(1)} %broadcast_multiply_fusion), kind=kOutput, calls=%fused_computation.45 | convolution fusion | flops 2876375040 | bytes 10476544 | tf_op jit(solution)/shard_map/sid,dce->csie/dot_general | solution.py:55
  56.0 1.5 copy-done.2
  57.7 1.3 fusion.63
  59.0 1.2 fusion.69
  60.4 2.0 copy.25
  63.4 1.3 slice_multiply_fusion.2
  64.8 72.3 %all-gather.7.cloned.1.call-done = bf16[4256,2,1,384]{3,1,2,0:T(2,128)(2,1)} async-done(((bf16[532,2,1,384]{3,1,2,0:T(2,128)(2,1)}), bf16[4256,2,1,384]{3,1,2,0:T(2,128)(2,1)}) %all-gather.7.cloned.1.call-update) | async-done | bytes 6537232 | tf_op jit(solution)/shard_map/all_gather | solution.py:87
  137.1 17.9 %copy.26 = bf16[4256,2,1,384]{0,3,1,2:T(8,128)(2,1)} copy(bf16[4256,2,1,384]{3,1,2,0:T(2,128)(2,1)} %all-gather.7.cloned.1.call-done) | data formatting | bytes 13074432 | tf_op jit(solution)/shard_map/all_gather | solution.py:87
  155.0 20.9 %fusion = (f32[6,512]{1,0:T(8,128)S(1)}, f32[6,512,4256]{1,2,0:T(8,128)}) fusion(f32[4256]{0:T(1024)S(1)} %fusion.93, bf16[4256,2,1,6,64]{0,4,3,2,1:T(8,128)(2,1)} %bitcast.108, f32[512,6,64]{0,2,1:T(8,128)S(1)} %bitcast.117, f32[64]{0:T(128)S(1)} %copy-done.5, f32[512,6]{0,1:T(8,128)S(1)} %add_rsqrt_fusion.1), kind=kOutput, calls=%fused_computation.2 | convolution fusion | flops 1713337344 | bytes 56468352 | tf_op jit(solution)/shard_map/sihd,kihd->ihsk/dot_general | solution.py:100
  175.9 17.1 %fusion.1 = f32[6,512]{1,0:T(8,128)S(1)} fusion(f32[6,512,4256]{1,2,0:T(8,128)} %get-tuple-element.16, f32[6,512]{1,0:T(8,128)S(1)} %get-tuple-element.15, f32[4256]{0:T(1024)S(1)} %fusion.93), kind=kLoop, calls=%fused_computation.3 | loop fusion | flops 52294656 | bytes 52339328 | tf_op jit(solution)/shard_map/reduce_sum | solution.py:105
  193.0 21.3 %fusion.59 = bf16[6,512,64]{1,2,0:T(8,128)(2,1)S(1)} fusion(f32[6,512,4256]{1,2,0:T(8,128)} %get-tuple-element.16, f32[6,512]{1,0:T(8,128)S(1)} %get-tuple-element.15, f32[4256]{0:T(1024)S(1)} %fusion.93, bf16[4256,2,1,6,64]{0,4,3,2,1:T(8,128)(2,1)} %bitcast.109, f32[6,512]{1,0:T(8,128)S(1)} %fusion.1), kind=kOutput, calls=%fused_computation.63 | convolution fusion | flops 1726218240 | bytes 56074880 | tf_op jit(solution)/shard_map/ihsk,kihd->ihsd/dot_general | solution.py:106
  214.4 3.0 fusion.15
  217.4 32.1 %reduce-scatter.3.cloned.1.call-done = bf16[128,1,2432]{2,0,1:T(8,128)(2,1)} async-done(((bf16[512,1,2432]{2,0,1:T(8,128)(2,1)}), bf16[128,1,2432]{2,0,1:T(8,128)(2,1)}) %reduce-scatter.3.cloned.1.call-update) | async-done | bytes 622608 | tf_op jit(solution)/shard_map/reduce_scatter | solution.py:114
  249.5 1.4 convert_reduce_fusion.1
  250.9 0.3 fusion.48
  251.2 1.3 fusion.51
  252.6 0.7 collective-permute-start
  253.3 0.3 collective-permute-start.1
  253.6 76.3 %all-gather.9.cloned.1.call-done = bf16[1024,1,2432]{2,0,1:T(8,128)(2,1)} async-done(((bf16[128,1,2432]{2,0,1:T(8,128)(2,1)}), bf16[1024,1,2432]{2,0,1:T(8,128)(2,1)}) %all-gather.9.cloned.1.call-update) | async-done | bytes 4980752 | tf_op jit(solution)/shard_map/all_gather | solution.py:128
  330.0 13.8 %fusion.67 = f32[1024,2432]{1,0:T(8,128)} fusion(bf16[608,2432]{1,0:T(8,128)(2,1)} %param.25, bf16[2432,608]{0,1:T(8,128)(2,1)} %param.24, bf16[1024,1,2432]{2,0,1:T(8,128)(2,1)} %all-gather.9.cloned.1.call-done), kind=kOutput, calls=%fused_computation.71 | convolution fusion | flops 6062178304 | bytes 20856832 | tf_op jit(solution)/shard_map/dot_general | solution.py:134
  343.8 14.4 %add_convert_fusion = bf16[1024,2432]{1,0:T(8,128)(2,1)} fusion(f32[1024,2432]{1,0:T(8,128)} %fusion.67, bf16[608,2432]{1,0:T(8,128)(2,1)} %collective-permute-done.1, bf16[2432,608]{0,1:T(8,128)(2,1)} %collective-permute-done, bf16[1024,1,2432]{2,0,1:T(8,128)(2,1)} %all-gather.9.cloned.1.call-done), kind=kOutput, calls=%fused_computation.6 | convolution fusion | flops 6067159040 | bytes 25837568 | tf_op jit(solution)/shard_map/dot_general | solution.py:134
  358.3 87.1 %reduce-scatter.5.cloned.1.call-done = bf16[128,2432]{1,0:T(8,128)(2,1)} async-done(((bf16[1024,2432]{1,0:T(8,128)(2,1)}), bf16[128,2432]{1,0:T(8,128)(2,1)}) %reduce-scatter.5.cloned.1.call-update) | async-done | bytes 622608 | tf_op jit(solution)/shard_map/reduce_scatter | solution.py:137
  445.4 2.1 fusion.52
  (47 shorter events, 1.7 us)
Async XLA Ops:
  6.5 207.8 %copy-start = (bf16[384,2432]{1,0:T(8,128)(2,1)S(1)}, bf16[384,2432]{1,0:T(8,128)(2,1)}, u32[]{:S(2)}) copy-start(bf16[384,2432]{1,0:T(8,128)(2,1)} %param.23) | copy-start | bytes 5603332
  6.5 40.1 %all-gather.5.cloned.1.call-start = ((), (), s32[]{:S(2)}) async-start(), calls=%async_computation.2 | async-start | bytes 3112960 | tf_op jit(solution)/shard_map/all_gather | solution.py:50
  7.3 129.8 %all-gather.7.cloned.1.call-start = ((), (), s32[]{:S(2)}) async-start(), calls=%async_computation.3 | async-start | bytes 7354368 | tf_op jit(solution)/shard_map/all_gather | solution.py:87
  13.1 3.8 copy-start.4
  46.6 2.5 copy-start.1
  55.9 1.5 copy-start.2
  62.4 187.1 %reduce-scatter.3.cloned.1.call-start = ((), (), s32[]{:S(2)}) async-start(), calls=%async_computation.4 | async-start | bytes 3112960 | tf_op jit(solution)/shard_map/reduce_scatter | solution.py:114
  64.8 90.2 %copy-start.5 = (f32[64]{0:T(128)S(1)}, f32[64]{0:T(128)}, u32[]{:S(2)}) copy-start(f32[64]{0:T(128)} %param.21) | copy-start | bytes 772
  214.4 35.1 %copy-start.3 = (bf16[8,16,1,2432]{3,1,2,0:T(8,128)(2,1)S(1)}, bf16[8,16,1,2432]{3,1,2,0:T(8,128)(2,1)}, u32[]{:S(2)}) copy-start(bf16[8,16,1,2432]{3,1,2,0:T(8,128)(2,1)} %param.13) | copy-start | bytes 1867780
  217.4 112.6 %all-gather.9.cloned.1.call-start = ((), (), s32[]{:S(2)}) async-start(), calls=%async_computation.6 | async-start | bytes 5603328 | tf_op jit(solution)/shard_map/all_gather | solution.py:128
  252.6 192.8 %reduce-scatter.5.cloned.1.call-start = ((), (), s32[]{:S(2)}) async-start(), calls=%async_computation.5 | async-start | bytes 5603328 | tf_op jit(solution)/shard_map/reduce_scatter | solution.py:137
  252.6 91.2 %collective-permute-start = (bf16[2432,608]{0,1:T(8,128)(2,1)}, bf16[2432,608]{0,1:T(8,128)(2,1)}, u32[]{:S(2)}, u32[]{:S(2)}) collective-permute-start(bf16[2432,608]{0,1:T(8,128)(2,1)} %param.24), channel_id=1, source_target_pairs={{0,32},{32,0},{1,33},{33,1},{2,34},{34,2},{3,35},{35,3},{4,36},{36... | collective-permute-start | bytes 8871944 | tf_op jit(solution)/shard_map/ppermute | solution.py:38
  253.3 90.5 %collective-permute-start.1 = (bf16[608,2432]{1,0:T(8,128)(2,1)}, bf16[608,2432]{1,0:T(8,128)(2,1)}, u32[]{:S(2)}, u32[]{:S(2)}) collective-permute-start(bf16[608,2432]{1,0:T(8,128)(2,1)} %param.25), channel_id=1, source_target_pairs={{0,32},{32,0},{1,33},{33,1},{2,34},{34,2},{3,35},{35,3},{4,36},{36... | collective-permute-start | bytes 8871944 | tf_op jit(solution)/shard_map/ppermute | solution.py:39
Sparse Core Ops, SparseCore 0:
  9.0 37.5 all-gather.4
  62.6 74.4 all-gather.6
  217.5 31.9 reduce-scatter.2
  252.7 77.2 all-gather.8
  358.4 86.9 reduce-scatter.4

commit v2 on v1

--- a/solution.py
+++ b/solution.py
@@ -34,9 +34,17 @@
     w_up,
     w_down,
 ):
-    swap = [(0, 1), (1, 0)]
-    other_up = lax.ppermute(w_up, "ic", swap)
-    other_down = lax.ppermute(w_down, "ic", swap)
+    n_row = lax.axis_size("row")
+    half_row = n_row // 2
+    mirror = []
+    for ih in range(2):
+        for y_lo in range(2):
+            for x in range(half_row):
+                mirror.append(
+                    (ih * n_row + y_lo * half_row + x, (1 - ih) * n_row + (1 - y_lo) * half_row + x)
+                )
+    other_up = lax.ppermute(w_up, ("ih", "row"), mirror)
+    other_down = lax.ppermute(w_down, ("ih", "row"), mirror)
 
     grid_rows, grid_cols, local_items, model_width = latents.shape
     own_rows = grid_rows * grid_cols
@@ -76,24 +84,24 @@
     )
     text_value = text_proj[1].astype(jnp.bfloat16)
 
-    piece_len = strip_len + text_len
-    kv_local = jnp.stack(
-        [
-            jnp.concatenate([key_img, text_key], axis=0),
-            jnp.concatenate([value_img, text_value], axis=0),
-        ],
-        axis=1,
-    )
+    text_slots = -(-text_len // 16) * 16
+    piece_len = strip_len + text_slots
+    pad = jnp.zeros((text_slots - text_len, local_items, head_cols), jnp.bfloat16)
+    kv_local = jnp.concatenate([key_img, text_key, pad, value_img, text_value, pad], axis=0)
     kv_all = lax.all_gather(kv_local, "row", axis=0, tiled=True)
-    n_keys = kv_all.shape[0]
-    kv_all = kv_all.reshape(n_keys, 2, local_items, local_heads, 64)
-    key_all = kv_all[:, 0]
-    value_all = kv_all[:, 1]
+    kv_all, other_up = lax.optimization_barrier((kv_all, other_up))
+    kv_all = kv_all.reshape(n_row, 2, piece_len, local_items, local_heads, 64)
+    n_keys = n_row * piece_len
+    key_all = kv_all[:, 0].reshape(n_keys, local_items, local_heads, 64)
+    value_all = kv_all[:, 1].reshape(n_keys, local_items, local_heads, 64)
 
     slot = jnp.arange(n_keys, dtype=jnp.int32)
     within = slot % piece_len
     text_pos = (slot // piece_len) * text_len + (within - strip_len)
-    live = (within < strip_len)[:, None] | (text_pos[:, None] < text_count[None, :])
+    is_text = (within >= strip_len) & (within < strip_len + text_len)
+    live = (within < strip_len)[:, None] | (
+        is_text[:, None] & (text_pos[:, None] < text_count[None, :])
+    )
     bias = jnp.where(live, 0.0, -jnp.inf).astype(jnp.float32)
 
     scores = (
@@ -111,6 +119,7 @@
     )
     heads_out = (accum / denom[..., None]).astype(jnp.bfloat16)
     attended = jnp.transpose(heads_out, (2, 0, 1, 3)).reshape(strip_len, local_items, head_cols)
+    attended, other_down = lax.optimization_barrier((attended, other_down))
     attn_out = lax.psum_scatter(
         jnp.einsum("sie,ed->sid", attended, w_out, preferred_element_type=jnp.float32).astype(
             jnp.bfloat16
@@ -125,7 +134,7 @@
     )
     flat_rows = normed_two.reshape(own_rows * local_items, model_width)
 
-    gathered = lax.all_gather(flat_rows, ("ih", "col"), axis=0, tiled=True)
+    gathered = lax.all_gather(flat_rows, ("ic", "col"), axis=0, tiled=True)
 
     def half(up, down):
         hidden = jax.nn.gelu(
@@ -136,7 +145,7 @@
     partial = half(w_up, w_down) + half(other_up, other_down)
     mlp_sum = lax.psum_scatter(
         partial.astype(jnp.bfloat16),
-        ("ih", "col"),
+        ("ic", "col"),
         scatter_dimension=0,
         tiled=True,
     ).astype(jnp.float32)

time: 455 us -> 469 us (1.031)
  local copies, waits for them, and re-layouts: 23.7 us -> 99.6 us
  waiting for transfers between devices: 298 us -> 226 us
  other arithmetic: 30.9 us -> 36.7 us
    all_gather x1, waiting for transfers between devices: 72.3 us -> 9.4 us  [local(): kv_all = lax.all_gather(kv_local, 'row', axis=0, tiled=True)]
    ppermute x2, waiting for transfers between devices: 0.01 us -> 61.6 us  [the longest x1 61.6 us: local(): other_up = lax.ppermute(w_up, ('ih', 'row'), mirror)]
    slice x0 -> x1, local copies, waits for them, and re-layouts: none -> 51.4 us  [local(): key_all = kv_all[:, 0].reshape(n_keys, local_items, local_heads, 64)]
    all_gather x1, waiting for transfers between devices: 76.3 us -> 35.7 us  [local(): gathered = lax.all_gather(flat_rows, ('ic', 'col'), axis=0, tiled=True)]
    reduce_scatter x1, waiting for transfers between devices: 87.1 us -> 59.4 us  [local(): lax.psum_scatter(partial.astype(jnp.bfloat16), ('ic', 'col'), scatter_dim...]
    all_gather x1 -> x0, local copies, waits for them, and re-layouts: 17.9 us -> none  [local(): kv_all = lax.all_gather(kv_local, 'row', axis=0, tiled=True)]
    reshape x0 -> x1, local copies, waits for them, and re-layouts: none -> 16.1 us  [local(): kv_all = kv_all.reshape(n_row, 2, piece_len, local_items, local_heads, 64)]
    another operation x1 -> x2, local copies, waits for them, and re-layouts: 2.04 us -> 14.8 us  [local(): jnp.stack([jnp.concatenate([key_img, text_key], axis=0), jnp.concatenate(...]
  transfers between devices with their start and end apart: 7 -> 7, of which waited for: 5 -> 6; matrix products, arithmetic and copies ran while one was open for 5% -> 36% of each run, Pallas kernels for 0% -> 0%
where the time goes in v2:
time: 469 us; the launch traced here: 467 us
  waiting for transfers between devices  226 us (48%)
  local copies, waits for them, and re-layouts  99.6 us (21%)
  matrix products  86.9 us (19%)
  other arithmetic  36.7 us (8%)
  between operations  14.7 us (3%)
    ppermute x1, waiting for transfers between devices, local(): other_up = lax.ppermute(w_up, ('ih', 'row'), mirror)  61.6 us
    reduce_scatter x1, waiting for transfers between devices, local(): lax.psum_scatter(partial.astype(jnp.bfloat16), ('ic', 'col'), scatter_dim...  59.4 us
    slice x1, local copies, waits for them, and re-layouts, local(): key_all = kv_all[:, 0].reshape(n_keys, local_items, local_heads, 64)  51.4 us
    all_gather x1, waiting for transfers between devices, local(): gathered = lax.all_gather(flat_rows, ('ic', 'col'), axis=0, tiled=True)  35.7 us
    reduce_scatter x1, waiting for transfers between devices, local(): lax.psum_scatter(jnp.einsum('sie,ed->sid', attended, w_out, preferred_ele...  32.1 us
    dot_general x2, matrix products, half(): return jnp.dot(hidden, down, preferred_element_type=jnp.float32)  28.2 us
    all_gather x1, waiting for transfers between devices, local(): strip_rows = lax.all_gather(tokens, 'col', axis=0, tiled=True)  27.5 us
    dot_general x1, matrix products, local(): jnp.einsum('sihd,kihd->ihsk', query, key_all, preferred_element_type=jnp....  22.6 us
  transfers between devices with their start and end apart: 7, of which 6 were waited for; matrix products, arithmetic and copies ran while one was open for 36% of the time, Pallas kernels for 0%

profile of v2, /device:TPU:1, one launch (start us, length us, event | category | flops | bytes accessed | tf_op | source)
XLA Modules:
  0.0 467.3 jit_solution(8386921645936212113)
XLA Ops:
  7.9 2.2 fusion.101
  12.0 1.1 fusion.75
  13.1 3.7 fusion.52
  19.1 27.5 %all-gather.5.cloned.1.call-done = bf16[512,1,2432]{2,0,1:T(8,128)(2,1)} async-done(((bf16[128,1,2432]{2,0,1:T(8,128)(2,1)}), bf16[512,1,2432]{2,0,1:T(8,128)(2,1)}) %all-gather.5.cloned.1.call-update) | async-done | bytes 2490384 | tf_op jit(solution)/shard_map/all_gather | solution.py:58
  46.6 2.3 convert_reduce_fusion
  49.8 6.1 %fusion.35 = f32[512,3,384]{0,2,1:T(8,128)S(1)} fusion(bf16[2432,3,384]{2,0,1:T(8,128)(2,1)} %param.19, bf16[512,1,2432]{2,0,1:T(8,128)(2,1)S(1)} %copy-done.1, f32[2432]{0:T(1024)S(1)} %get-tuple-element.18, f32[2432]{0:T(1024)S(1)} %get-tuple-element.19, f32[512]{0:T(512)S(1)} %add_rsqrt_fusion.3, f32[512]{0:T(512)S(1)} %broadcast_multiply_fusion), kind=kOutput, calls=%fused_computation.44 | convolution fusion | flops 2876375040 | bytes 10476544 | tf_op jit(solution)/shard_map/sid,dce->csie/dot_general | solution.py:63
  56.0 1.5 copy-done.2
  57.7 1.3 fusion.62
  59.0 1.2 fusion.69
  60.8 1.4 concatenate.3
  62.2 1.3 copy.38
  63.6 2.5 collective-permute-start
  67.1 1.3 slice_multiply_fusion.2
  68.6 61.6 %collective-permute-done = bf16[2432,608]{0,1:T(8,128)(2,1)} collective-permute-done((bf16[2432,608]{0,1:T(8,128)(2,1)}, bf16[2432,608]{0,1:T(8,128)(2,1)}, u32[]{:S(2)}, u32[]{:S(2)}) %collective-permute-start) | collective-permute-done | bytes 2957344 | tf_op jit(solution)/shard_map/ppermute | solution.py:46
  130.2 9.4 %all-gather.7.cloned.1.call-done = bf16[8704,1,384]{2,0,1:T(8,128)(2,1)} async-done(((bf16[1088,1,384]{2,0,1:T(8,128)(2,1)}), bf16[8704,1,384]{2,0,1:T(8,128)(2,1)}) %all-gather.7.cloned.1.call-update) | async-done | bytes 6684688 | tf_op jit(solution)/shard_map/all_gather | solution.py:91
  139.6 9.5 %copy.39 = bf16[8704,1,384]{0,2,1:T(8,128)(2,1)} copy(bf16[8704,1,384]{2,0,1:T(8,128)(2,1)} %all-gather.7.cloned.1.call-done) | data formatting | bytes 13369344 | tf_op jit(solution)/shard_map/optimization_barrier | solution.py:92
  149.1 16.1 %reshape.432 = bf16[8,2,544,1,6,64]{2,1,0,5,4,3:T(2,128)(2,1)} reshape(bf16[8704,1,384]{0,2,1:T(8,128)(2,1)} %copy.39) | data formatting | bytes 13369344 | tf_op jit(solution)/shard_map/reshape | solution.py:93
  165.2 51.4 %slice_reduce_fusion.1 = (bf16[8,544,6,64]{1,0,3,2:T(8,128)(2,1)}, bf16[8,544,6,64]{1,0,3,2:T(8,128)(2,1)}) fusion(bf16[8,2,544,1,6,64]{2,1,0,5,4,3:T(2,128)(2,1)} %reshape.432), kind=kLoop, calls=%fused_computation.8 | loop fusion | bytes 13369344 | tf_op jit(solution)/shard_map/slice | solution.py:95
  216.6 7.4 %reshape.433 = bf16[4352,6,64]{0,2,1:T(8,128)(2,1)} reshape(bf16[8,544,6,64]{1,0,3,2:T(8,128)(2,1)} %get-tuple-element.13) | data formatting | bytes 6684672 | tf_op jit(solution)/shard_map/reshape.29
  224.0 22.6 %fusion = (f32[6,512]{1,0:T(8,128)S(1)}, f32[6,512,4352]{2,1,0:T(8,128)}) fusion(f32[4352]{0:T(1024)S(1)} %fusion.97, bf16[4352,6,64]{0,2,1:T(8,128)(2,1)} %reshape.433, f32[512,6,64]{0,2,1:T(8,128)S(1)} %bitcast.109, f32[64]{0:T(128)S(1)} %copy-done.8, f32[512,6]{0,1:T(8,128)S(1)} %add_rsqrt_fusion.1), kind=kOutput, calls=%fused_computation.2 | convolution fusion | flops 1751970816 | bytes 57648384 | tf_op jit(solution)/shard_map/sihd,kihd->ihsk/dot_general | solution.py:108
  246.6 21.9 %fusion.1 = f32[6,512]{1,0:T(8,128)S(1)} fusion(f32[6,512,4352]{2,1,0:T(8,128)} %get-tuple-element.26, f32[6,512]{1,0:T(8,128)S(1)} %get-tuple-element.25, f32[4352]{0:T(1024)S(1)} %fusion.97), kind=kLoop, calls=%fused_computation.3 | loop fusion | flops 53474304 | bytes 53519360 | tf_op jit(solution)/shard_map/reduce_sum | solution.py:113
  268.6 7.4 %reshape.434 = bf16[4352,6,64]{0,2,1:T(8,128)(2,1)} reshape(bf16[8,544,6,64]{1,0,3,2:T(8,128)(2,1)} %get-tuple-element.14) | data formatting | bytes 6684672 | tf_op jit(solution)/shard_map/reshape.35
  276.0 21.0 %fusion.58 = bf16[6,512,64]{1,2,0:T(8,128)(2,1)S(1)} fusion(bf16[4352,6,64]{0,2,1:T(8,128)(2,1)} %reshape.434, f32[6,512,4352]{2,1,0:T(8,128)} %get-tuple-element.26, f32[6,512]{1,0:T(8,128)S(1)} %get-tuple-element.25, f32[4352]{0:T(1024)S(1)} %fusion.97, f32[6,512]{1,0:T(8,128)S(1)} %fusion.1), kind=kOutput, calls=%fused_computation.62 | convolution fusion | flops 1765146624 | bytes 57254912 | tf_op jit(solution)/shard_map/ihsk,kihd->ihsd/dot_general | solution.py:114
  297.0 3.0 fusion.15
  300.1 32.1 %reduce-scatter.3.cloned.1.call-done = bf16[128,1,2432]{2,0,1:T(8,128)(2,1)} async-done(((bf16[512,1,2432]{2,0,1:T(8,128)(2,1)}), bf16[128,1,2432]{2,0,1:T(8,128)(2,1)}) %reduce-scatter.3.cloned.1.call-update) | async-done | bytes 622608 | tf_op jit(solution)/shard_map/reduce_scatter | solution.py:123
  332.2 1.4 convert_reduce_fusion.1
  333.9 1.3 fusion.50
  335.3 35.7 %all-gather.9.cloned.1.call-done = bf16[1024,1,2432]{2,0,1:T(8,128)(2,1)} async-done(((bf16[128,1,2432]{2,0,1:T(8,128)(2,1)}), bf16[1024,1,2432]{2,0,1:T(8,128)(2,1)}) %all-gather.9.cloned.1.call-update) | async-done | bytes 4980752 | tf_op jit(solution)/shard_map/all_gather | solution.py:137
  371.0 13.8 %fusion.66 = f32[1024,2432]{1,0:T(8,128)} fusion(bf16[608,2432]{1,0:T(8,128)(2,1)} %param.25, bf16[2432,608]{0,1:T(8,128)(2,1)} %param.24, bf16[1024,1,2432]{2,0,1:T(8,128)(2,1)} %all-gather.9.cloned.1.call-done), kind=kOutput, calls=%fused_computation.69 | convolution fusion | flops 6062178304 | bytes 20856832 | tf_op jit(solution)/shard_map/dot_general | solution.py:143
  384.8 14.4 %add_convert_fusion = bf16[1024,2432]{1,0:T(8,128)(2,1)} fusion(f32[1024,2432]{1,0:T(8,128)} %fusion.66, bf16[608,2432]{1,0:T(8,128)(2,1)} %collective-permute-done.1, bf16[2432,608]{0,1:T(8,128)(2,1)} %collective-permute-done, bf16[1024,1,2432]{2,0,1:T(8,128)(2,1)} %all-gather.9.cloned.1.call-done), kind=kOutput, calls=%fused_computation.6 | convolution fusion | flops 6067159040 | bytes 25837568 | tf_op jit(solution)/shard_map/dot_general | solution.py:143
  399.2 59.4 %reduce-scatter.5.cloned.1.call-done = bf16[128,2432]{1,0:T(8,128)(2,1)} async-done(((bf16[1024,2432]{1,0:T(8,128)(2,1)}), bf16[128,2432]{1,0:T(8,128)(2,1)}) %reduce-scatter.5.cloned.1.call-update) | async-done | bytes 622608 | tf_op jit(solution)/shard_map/reduce_scatter | solution.py:146
  458.7 2.1 fusion.51
  (57 shorter events, 7.6 us)
Async XLA Ops:
  6.5 290.5 %copy-start = (bf16[384,2432]{1,0:T(8,128)(2,1)S(1)}, bf16[384,2432]{1,0:T(8,128)(2,1)}, u32[]{:S(2)}) copy-start(bf16[384,2432]{1,0:T(8,128)(2,1)} %param.23) | copy-start | bytes 5603332
  6.5 40.1 %all-gather.5.cloned.1.call-start = ((), (), s32[]{:S(2)}) async-start(), calls=%async_computation.2 | async-start | bytes 3112960 | tf_op jit(solution)/shard_map/all_gather | solution.py:58
  7.3 132.3 %all-gather.7.cloned.1.call-start = ((), (), s32[]{:S(2)}) async-start(), calls=%async_computation.3 | async-start | bytes 7520256 | tf_op jit(solution)/shard_map/all_gather | solution.py:91
  13.1 3.8 copy-start.4
  46.6 2.5 copy-start.1
  55.9 1.5 copy-start.2
  63.6 268.6 %reduce-scatter.3.cloned.1.call-start = ((), (), s32[]{:S(2)}) async-start(), calls=%async_computation.4 | async-start | bytes 3112960 | tf_op jit(solution)/shard_map/reduce_scatter | solution.py:123
  63.6 66.5 %collective-permute-start = (bf16[2432,608]{0,1:T(8,128)(2,1)}, bf16[2432,608]{0,1:T(8,128)(2,1)}, u32[]{:S(2)}, u32[]{:S(2)}) collective-permute-start(bf16[2432,608]{0,1:T(8,128)(2,1)} %param.24), channel_id=1, source_target_pairs={{0,80},{4,84},{8,88},{12,92},{16,64},{20,68},{24,72},{28,76},{64,1... | collective-permute-start | bytes 8871944 | tf_op jit(solution)/shard_map/ppermute | solution.py:46
  66.2 230.8 %collective-permute-start.1 = (bf16[608,2432]{1,0:T(8,128)(2,1)}, bf16[608,2432]{1,0:T(8,128)(2,1)}, u32[]{:S(2)}, u32[]{:S(2)}) collective-permute-start(bf16[608,2432]{1,0:T(8,128)(2,1)} %param.25), channel_id=1, source_target_pairs={{0,80},{4,84},{8,88},{12,92},{16,64},{20,68},{24,72},{28,76},{64,1... | collective-permute-start | bytes 8871944 | tf_op jit(solution)/shard_map/ppermute | solution.py:47
  216.6 7.4 %copy-start.8 = (f32[64]{0:T(128)S(1)}, f32[64]{0:T(128)}, u32[]{:S(2)}) copy-start(f32[64]{0:T(128)} %param.21) | copy-start | bytes 772
  297.0 35.2 %copy-start.3 = (bf16[8,16,1,2432]{3,1,2,0:T(8,128)(2,1)S(1)}, bf16[8,16,1,2432]{3,1,2,0:T(8,128)(2,1)}, u32[]{:S(2)}) copy-start(bf16[8,16,1,2432]{3,1,2,0:T(8,128)(2,1)} %param.13) | copy-start | bytes 1867780
  297.0 35.2 %copy-start.7 = (f32[2432]{0:T(1024)S(1)}, f32[2432]{0:T(1024)}, u32[]{:S(2)}) copy-start(f32[2432]{0:T(1024)} %get-tuple-element.20) | copy-start | bytes 29188
  300.0 33.9 %copy-start.5 = (f32[2432]{0:T(1024)S(1)}, f32[2432]{0:T(1024)}, u32[]{:S(2)}) copy-start(f32[2432]{0:T(1024)} %get-tuple-element.16) | copy-start | bytes 29188
  300.0 33.9 %copy-start.6 = (f32[2432]{0:T(1024)S(1)}, f32[2432]{0:T(1024)}, u32[]{:S(2)}) copy-start(f32[2432]{0:T(1024)} %get-tuple-element.17) | copy-start | bytes 29188
  300.1 70.9 %all-gather.9.cloned.1.call-start = ((), (), s32[]{:S(2)}) async-start(), calls=%async_computation.6 | async-start | bytes 5603328 | tf_op jit(solution)/shard_map/all_gather | solution.py:137
  335.3 123.4 %reduce-scatter.5.cloned.1.call-start = ((), (), s32[]{:S(2)}) async-start(), calls=%async_computation.5 | async-start | bytes 5603328 | tf_op jit(solution)/shard_map/reduce_scatter | solution.py:146
Sparse Core Ops, SparseCore 0:
  9.0 37.5 all-gather.4
  63.7 75.8 all-gather.6
  300.2 31.9 reduce-scatter.2
  335.4 35.5 all-gather.8
  399.4 59.2 reduce-scatter.4

commit v3 on v2

--- a/solution.py
+++ b/solution.py
@@ -1,6 +1,8 @@
 import jax
 import jax.numpy as jnp
 from jax import lax
+from jax.experimental import pallas as pl
+from jax.experimental.pallas import tpu as pltpu
 from jax.sharding import Mesh
 from jax.sharding import PartitionSpec as P
 
@@ -17,6 +19,57 @@
 
 def rms_heads(values, gain):
     return values * lax.rsqrt(jnp.mean(values * values, axis=-1, keepdims=True) + epsilon) * gain
+
+
+def attention_kernel(q_ref, *refs):
+    kv_refs = refs[:-3]
+    bias_ref, o_ref, s_scr = refs[-3:]
+    n_strip = len(kv_refs)
+    width = q_ref.shape[1]
+    piece = s_scr.shape[2]
+    q = q_ref[...]
+    tq = q.shape[0]
+    lane = lax.broadcasted_iota(jnp.int32, (tq, width), 1)
+    half = width // 2
+    outs = []
+    for parity in range(2):
+        own = (lane >= parity * half) & (lane < (parity + 1) * half)
+        q_one = jnp.where(own, q, jnp.zeros_like(q))
+        row_max = jnp.full((tq, 1), -jnp.inf, jnp.float32)
+        for r in range(n_strip):
+            keys = kv_refs[r][0:piece, :]
+            s = lax.dot_general(q_one, keys, (((1,), (1,)), ((), ())),
+                                preferred_element_type=jnp.float32)
+            s = s * 0.125 + bias_ref[r:r + 1, :]
+            s_scr[r] = s
+            row_max = jnp.maximum(row_max, jnp.max(s, axis=1, keepdims=True))
+        denom = jnp.zeros((tq, 1), jnp.float32)
+        acc = jnp.zeros((tq, width), jnp.float32)
+        for r in range(n_strip):
+            w = jnp.exp(s_scr[r] - row_max)
+            denom = denom + jnp.sum(w, axis=1, keepdims=True)
+            acc = acc + jnp.dot(w.astype(jnp.bfloat16), kv_refs[r][piece:2 * piece, :],
+                                preferred_element_type=jnp.float32)
+        outs.append(acc / denom)
+    o_ref[...] = jnp.where(lane < half, outs[0], outs[1]).astype(o_ref.dtype)
+
+
+def attention(query, kv_parts, bias, tq=512):
+    S, C = query.shape
+    two_piece = kv_parts[0].shape[0]
+    piece = two_piece // 2
+    R = len(kv_parts)
+    pairs = C // 128
+    return pl.pallas_call(
+        attention_kernel,
+        out_shape=jax.ShapeDtypeStruct((S, C), jnp.bfloat16),
+        grid=(pairs, S // tq),
+        in_specs=[pl.BlockSpec((tq, 128), lambda h, i: (i, h))]
+        + [pl.BlockSpec((two_piece, 128), lambda h, i: (0, h)) for _ in range(R)]
+        + [pl.BlockSpec((R, piece), lambda h, i: (0, 0))],
+        out_specs=pl.BlockSpec((tq, 128), lambda h, i: (i, h)),
+        scratch_shapes=[pltpu.VMEM((R, tq, piece), jnp.float32)],
+    )(query, *kv_parts, bias)
 
 
 def local(
@@ -44,7 +97,9 @@
                     (ih * n_row + y_lo * half_row + x, (1 - ih) * n_row + (1 - y_lo) * half_row + x)
                 )
     other_up = lax.ppermute(w_up, ("ih", "row"), mirror)
-    other_down = lax.ppermute(w_down, ("ih", "row"), mirror)
+    down_rows = w_down.shape[0] // 2
+    other_down_a = lax.ppermute(w_down[:down_rows], ("ih", "row"), mirror)
+    other_down_b = lax.ppermute(w_down[down_rows:], ("ih", "row"), mirror)
 
     grid_rows, grid_cols, local_items, model_width = latents.shape
     own_rows = grid_rows * grid_cols
@@ -86,40 +141,32 @@
 
     text_slots = -(-text_len // 16) * 16
     piece_len = strip_len + text_slots
-    pad = jnp.zeros((text_slots - text_len, local_items, head_cols), jnp.bfloat16)
-    kv_local = jnp.concatenate([key_img, text_key, pad, value_img, text_value, pad], axis=0)
-    kv_all = lax.all_gather(kv_local, "row", axis=0, tiled=True)
-    kv_all, other_up = lax.optimization_barrier((kv_all, other_up))
-    kv_all = kv_all.reshape(n_row, 2, piece_len, local_items, local_heads, 64)
-    n_keys = n_row * piece_len
-    key_all = kv_all[:, 0].reshape(n_keys, local_items, local_heads, 64)
-    value_all = kv_all[:, 1].reshape(n_keys, local_items, local_heads, 64)
-
-    slot = jnp.arange(n_keys, dtype=jnp.int32)
-    within = slot % piece_len
-    text_pos = (slot // piece_len) * text_len + (within - strip_len)
-    is_text = (within >= strip_len) & (within < strip_len + text_len)
-    live = (within < strip_len)[:, None] | (
-        is_text[:, None] & (text_pos[:, None] < text_count[None, :])
+    flat_kv = [
+        part.reshape(part.shape[0], local_items * head_cols)
+        for part in (key_img, text_key, value_img, text_value)
+    ]
+    pad = jnp.zeros((text_slots - text_len, local_items * head_cols), jnp.bfloat16)
+    kv_local = jnp.concatenate(
+        [flat_kv[0], flat_kv[1], pad, flat_kv[2], flat_kv[3], pad], axis=0
+    )
+    me = lax.axis_index("row")
+    kv_parts = [kv_local] + [
+        lax.ppermute(kv_local, "row", [(i, (i + k) % n_row) for i in range(n_row)])
+        for k in range(1, n_row)
+    ]
+    kv_parts, other_up = lax.optimization_barrier((kv_parts, other_up))
+
+    within = jnp.arange(piece_len, dtype=jnp.int32)[None, :]
+    strip_of = (me - jnp.arange(n_row, dtype=jnp.int32)) % n_row
+    text_pos = strip_of[:, None] * text_len + (within - strip_len)
+    live = (within < strip_len) | (
+        (within < strip_len + text_len) & (text_pos < text_count[0])
     )
     bias = jnp.where(live, 0.0, -jnp.inf).astype(jnp.float32)
 
-    scores = (
-        jnp.einsum("sihd,kihd->ihsk", query, key_all, preferred_element_type=jnp.float32) * 0.125
-    )
-    scores = scores + jnp.transpose(bias)[:, None, None, :]
-    row_max = jnp.max(scores, axis=-1, keepdims=True)
-    probs = jnp.exp(scores - row_max)
-    denom = jnp.sum(probs, axis=-1)
-    accum = jnp.einsum(
-        "ihsk,kihd->ihsd",
-        probs.astype(jnp.bfloat16),
-        value_all,
-        preferred_element_type=jnp.float32,
-    )
-    heads_out = (accum / denom[..., None]).astype(jnp.bfloat16)
-    attended = jnp.transpose(heads_out, (2, 0, 1, 3)).reshape(strip_len, local_items, head_cols)
-    attended, other_down = lax.optimization_barrier((attended, other_down))
+    heads_out = attention(query.reshape(strip_len, head_cols), kv_parts, bias)
+    heads_out, other_down_a = lax.optimization_barrier((heads_out, other_down_a))
+    attended = heads_out.reshape(strip_len, local_items, head_cols)
     attn_out = lax.psum_scatter(
         jnp.einsum("sie,ed->sid", attended, w_out, preferred_element_type=jnp.float32).astype(
             jnp.bfloat16
@@ -128,6 +175,8 @@
         scatter_dimension=0,
         tiled=True,
     ).astype(jnp.float32)
+    attn_out, other_down_b = lax.optimization_barrier((attn_out, other_down_b))
+    other_down = jnp.concatenate([other_down_a, other_down_b], axis=0)
     residual = (tokens.astype(jnp.float32) + modulation[:, 2] * attn_out).astype(jnp.bfloat16)
     normed_two = (layer_norm(residual) * (1.0 + modulation[:, 4]) + modulation[:, 3]).astype(
         jnp.bfloat16
@@ -143,12 +192,12 @@
         return jnp.dot(hidden, down, preferred_element_type=jnp.float32)
 
     partial = half(w_up, w_down) + half(other_up, other_down)
-    mlp_sum = lax.psum_scatter(
-        partial.astype(jnp.bfloat16),
-        ("ic", "col"),
-        scatter_dimension=0,
-        tiled=True,
-    ).astype(jnp.float32)
+    chip_sum = lax.psum_scatter(
+        partial.astype(jnp.bfloat16), "ic", scatter_dimension=0, tiled=True
+    )
+    mlp_sum = lax.psum_scatter(chip_sum, "col", scatter_dimension=0, tiled=True).astype(
+        jnp.float32
+    )
     mlp_sum = mlp_sum.reshape(own_rows, local_items, model_width)
     updated = (residual.astype(jnp.float32) + modulation[:, 5] * mlp_sum).astype(jnp.bfloat16)
     return updated.reshape(grid_rows, grid_cols, local_items, model_width)

time: 469 us -> 361 us (0.77)
  local copies, waits for them, and re-layouts: 99.6 us -> 13.5 us
  matrix products: 86.9 us -> 44.4 us
  Pallas kernels: 0 us -> 24.6 us
  other arithmetic: 36.7 us -> 13.9 us
  starting transfers between devices: 2.99 us -> 14.8 us
  waiting for transfers between devices: 226 us -> 234 us
    ppermute x1 -> x9, waiting for transfers between devices: 0.01 us -> 92.6 us  [the longest x7 88.6 us: local(): lax.ppermute(kv_local, 'row', [(i, (i + k) % n_row) for i in range(n_row)])]
    ppermute x1, waiting for transfers between devices: 61.6 us -> 0.01 us  [local(): other_up = lax.ppermute(w_up, ('ih', 'row'), mirror)]
    slice x1, local copies, waits for them, and re-layouts: 51.4 us -> 3.61 us  [local(): other_down_b = lax.ppermute(w_down[down_rows:], ('ih', 'row'), mirror)]
    dot_general x2 -> x1, matrix products: 43.7 us -> 7.26 us  [half(): jnp.dot(gathered, up, preferred_element_type=jnp.float32)]
    pallas_call x0 -> x1, Pallas kernels: none -> 24.6 us  [attention(): pl.pallas_call(attention_kernel, out_shape=jax.ShapeDtypeStruct((S, C), j...]
    reduce_sum x1 -> x0, other arithmetic: 21.9 us -> none  [local(): denom = jnp.sum(probs, axis=-1)]
    reshape x1 -> x0, local copies, waits for them, and re-layouts: 16.1 us -> none  [local(): kv_all = kv_all.reshape(n_row, 2, piece_len, local_items, local_heads, 64)]
    another operation x2 -> x0, local copies, waits for them, and re-layouts: 14.8 us -> none
  transfers between devices with their start and end apart: 7 -> 15, of which waited for: 6 -> 10; matrix products, arithmetic and copies ran while one was open for 36% -> 9% of each run, Pallas kernels for 0% -> 7%
where the time goes in v3:
time: 361 us; the launch traced here: 360 us
  waiting for transfers between devices  234 us (65%)
  matrix products  44.4 us (12%)
  Pallas kernels  24.6 us (7%)
  starting transfers between devices  14.8 us (4%)
  between operations  14.8 us (4%)
  other arithmetic  13.9 us (4%)
  local copies, waits for them, and re-layouts  13.5 us (4%)
    ppermute x7, waiting for transfers between devices, local(): lax.ppermute(kv_local, 'row', [(i, (i + k) % n_row) for i in range(n_row)])  88.6 us
    reduce_scatter x1, waiting for transfers between devices, local(): lax.psum_scatter(chip_sum, 'col', scatter_dimension=0, tiled=True)  36.6 us
    all_gather x1, waiting for transfers between devices, local(): gathered = lax.all_gather(flat_rows, ('ic', 'col'), axis=0, tiled=True)  32.7 us
    reduce_scatter x1, waiting for transfers between devices, local(): lax.psum_scatter(jnp.einsum('sie,ed->sid', attended, w_out, preferred_ele...  29.3 us
    all_gather x1, waiting for transfers between devices, local(): strip_rows = lax.all_gather(tokens, 'col', axis=0, tiled=True)  26.9 us
    pallas_call x1, Pallas kernels, attention(): pl.pallas_call(attention_kernel, out_shape=jax.ShapeDtypeStruct((S, C), j...  24.6 us
    dot_general x2, matrix products, half(): return jnp.dot(hidden, down, preferred_element_type=jnp.float32)  21.9 us
    reduce_scatter x1, waiting for transfers between devices, local(): lax.psum_scatter(partial.astype(jnp.bfloat16), 'ic', scatter_dimension=0,...  15.5 us
  transfers between devices with their start and end apart: 15, of which 10 were waited for; matrix products, arithmetic and copies ran while one was open for 9% of the time, Pallas kernels for 7%

profile of v3, /device:TPU:1, one launch (start us, length us, event | category | flops | bytes accessed | tf_op | source)
XLA Modules:
  0.0 360.4 jit_solution(4939381614971276468)
XLA Ops:
  7.3 3.6 %collective-permute-start.7 = (bf16[2432,608]{0,1:T(8,128)(2,1)}, bf16[2432,608]{0,1:T(8,128)(2,1)}, u32[]{:S(2)}, u32[]{:S(2)}) collective-permute-start(bf16[2432,608]{0,1:T(8,128)(2,1)} %param.24), channel_id=1, source_target_pairs={{0,80},{4,84},{8,88},{12,92},{16,64},{20,68},{24,72},{28,76},{64,1... | collective-permute-start | bytes 8871944 | tf_op jit(solution)/shard_map/ppermute | solution.py:99
  13.1 2.2 fusion.80
  15.7 2.7 fusion.53
  19.6 26.9 %all-gather.4.cloned.1.call-done = bf16[512,1,2432]{2,0,1:T(8,128)(2,1)} async-done(((bf16[128,1,2432]{2,0,1:T(8,128)(2,1)}), bf16[512,1,2432]{2,0,1:T(8,128)(2,1)}) %all-gather.4.cloned.1.call-update) | async-done | bytes 2490384 | tf_op jit(solution)/shard_map/all_gather | solution.py:113
  46.6 2.3 convert_reduce_fusion
  49.8 6.4 %fusion.39 = f32[3,512,1,384]{3,1,2,0:T(8,128)S(1)} fusion(bf16[2432,3,384]{2,0,1:T(8,128)(2,1)} %param.19, bf16[512,1,2432]{2,0,1:T(8,128)(2,1)S(1)} %copy-done.2, f32[2432]{0:T(1024)S(1)} %get-tuple-element.34, f32[2432]{0:T(1024)S(1)} %get-tuple-element.35, f32[512]{0:T(512)S(1)} %add_rsqrt_fusion.3, f32[512]{0:T(512)S(1)} %broadcast_multiply_fusion), kind=kOutput, calls=%fused_computation.47 | convolution fusion | flops 2876375040 | bytes 10476544 | tf_op jit(solution)/shard_map/sid,dce->csie/dot_general | solution.py:118
  56.3 1.4 copy-done.3
  59.4 1.4 copy.20
  61.0 1.2 copy.21
  62.2 1.2 fusion.63
  63.4 2.5 fusion.57
  66.7 3.4 collective-permute-start.6
  71.2 3.6 %fusion.92 = (bf16[304,2432]{1,0:T(8,128)(2,1)}, bf16[304,2432]{1,0:T(8,128)(2,1)}) fusion(bf16[608,2432]{1,0:T(8,128)(2,1)} %param.25), kind=kLoop, calls=%fused_computation.124 | loop fusion | bytes 5914624 | tf_op jit(solution)/shard_map/slice | solution.py:102
  74.9 2.5 collective-permute-start.8
  77.3 36.7 %collective-permute-done.6.refs_7_ = bf16[1088,384]{1,0:T(8,128)(2,1)S(1)} collective-permute-done((bf16[1088,384]{1,0:T(8,128)(2,1)S(1)}, bf16[1088,384]{1,0:T(8,128)(2,1)S(1)}, u32[]{:S(2)}, u32[]{:S(2)}) %collective-permute-start.6) | collective-permute-done | bytes 835616 | tf_op jit(solution)/shard_map/ppermute | solution.py:154
  114.1 3.7 %collective-permute-start = (bf16[1088,384]{1,0:T(8,128)(2,1)S(1)}, bf16[1088,384]{1,0:T(8,128)(2,1)}, u32[]{:S(2)}, u32[]{:S(2)}) collective-permute-start(bf16[1088,384]{1,0:T(8,128)(2,1)S(1)} %concatenate.6.refs_0_), channel_id=1, source_target_pairs={{0,4},{4,8},{8,12},{12,16},{16,20},{20,24},{24,28},{28,0},{1,5},{5... | collective-permute-start | bytes 2506760 | tf_op jit(solution)/shard_map/ppermute | solution.py:154
  119.2 20.5 %collective-permute-done.2.refs_3_ = bf16[1088,384]{1,0:T(8,128)(2,1)} collective-permute-done((bf16[1088,384]{1,0:T(8,128)(2,1)S(1)}, bf16[1088,384]{1,0:T(8,128)(2,1)}, u32[]{:S(2)}, u32[]{:S(2)}) %collective-permute-start.2) | collective-permute-done | bytes 835616 | tf_op jit(solution)/shard_map/ppermute | solution.py:154
  139.7 12.3 %collective-permute-done.1.refs_2_ = bf16[1088,384]{1,0:T(8,128)(2,1)} collective-permute-done((bf16[1088,384]{1,0:T(8,128)(2,1)S(1)}, bf16[1088,384]{1,0:T(8,128)(2,1)}, u32[]{:S(2)}, u32[]{:S(2)}) %collective-permute-start.1) | collective-permute-done | bytes 835616 | tf_op jit(solution)/shard_map/ppermute | solution.py:154
  152.1 19.0 %collective-permute-done.refs_1_ = bf16[1088,384]{1,0:T(8,128)(2,1)} collective-permute-done((bf16[1088,384]{1,0:T(8,128)(2,1)S(1)}, bf16[1088,384]{1,0:T(8,128)(2,1)}, u32[]{:S(2)}, u32[]{:S(2)}) %collective-permute-start) | collective-permute-done | bytes 835616 | tf_op jit(solution)/shard_map/ppermute | solution.py:154
  171.1 24.6 %shard_map.127 = bf16[512,384]{1,0:T(8,128)(2,1)} custom-call(bf16[512,384]{1,0:T(8,128)(2,1)} %get-tuple-element.42.q_ref, bf16[1088,384]{1,0:T(8,128)(2,1)} %copy-done.4, bf16[1088,384]{1,0:T(8,128)(2,1)} %collective-permute-done.refs_1_, bf16[1088,384]{1,0:T(8,128)(2,1)} %collective-permute-done.1.refs_2_, ...), custom_call_target="tpu_custom_call" | custom-call | tf_op jit(solution)/shard_map/pallas_call | solution.py:63
  195.7 3.9 %fusion.10 = bf16[512,1,2432]{2,0,1:T(8,128)(2,1)} fusion(bf16[512,384]{1,0:T(8,128)(2,1)} %shard_map.127, bf16[384,2432]{1,0:T(8,128)(2,1)S(1)} %copy-done), kind=kOutput, calls=%fused_computation.14 | convolution fusion | flops 957546496 | bytes 4751360 | tf_op jit(solution)/shard_map/sie,ed->sid/dot_general | solution.py:171
  199.7 1.3 copy-done.6
  201.0 29.3 %reduce-scatter.4.cloned.1.call-done = bf16[128,1,2432]{2,0,1:T(8,128)(2,1)} async-done(((bf16[512,1,2432]{2,0,1:T(8,128)(2,1)}), bf16[128,1,2432]{2,0,1:T(8,128)(2,1)}) %reduce-scatter.4.cloned.1.call-update) | async-done | bytes 622608 | tf_op jit(solution)/shard_map/reduce_scatter | solution.py:170
  231.4 4.0 %collective-permute-done.9 = bf16[304,2432]{1,0:T(8,128)(2,1)} collective-permute-done((bf16[304,2432]{1,0:T(8,128)(2,1)S(1)}, bf16[304,2432]{1,0:T(8,128)(2,1)}, u32[]{:S(2)}, u32[]{:S(2)}) %collective-permute-start.9) | collective-permute-done | bytes 1478688 | tf_op jit(solution)/shard_map/ppermute | solution.py:102
  236.1 1.3 fusion.51
  237.7 32.7 %all-gather.6.cloned.1.call-done = bf16[1024,1,2432]{2,0,1:T(8,128)(2,1)} async-done(((bf16[128,1,2432]{2,0,1:T(8,128)(2,1)}), bf16[1024,1,2432]{2,0,1:T(8,128)(2,1)}) %all-gather.6.cloned.1.call-update) | async-done | bytes 4980752 | tf_op jit(solution)/shard_map/all_gather | solution.py:186
  270.4 13.8 %fusion.61 = f32[1024,2432]{1,0:T(8,128)} fusion(bf16[608,2432]{1,0:T(8,128)(2,1)} %param.25, bf16[2432,608]{0,1:T(8,128)(2,1)} %param.24, bf16[1024,1,2432]{2,0,1:T(8,128)(2,1)} %all-gather.6.cloned.1.call-done), kind=kOutput, calls=%fused_computation.66 | convolution fusion | flops 6062178304 | bytes 20856832 | tf_op jit(solution)/shard_map/dot_general | solution.py:192
  284.2 7.3 %fusion.31 = bf16[1024,608]{0,1:T(8,128)(2,1)S(1)} fusion(bf16[2432,608]{0,1:T(8,128)(2,1)} %collective-permute-done.7, bf16[1024,1,2432]{2,0,1:T(8,128)(2,1)} %all-gather.6.cloned.1.call-done), kind=kOutput, calls=%fused_computation.37 | convolution fusion | flops 3033890816 | bytes 9183232 | tf_op jit(solution)/shard_map/dot_general | solution.py:190
  291.5 8.1 %add_convert_fusion = bf16[1024,2432]{1,0:T(8,128)(2,1)} fusion(f32[1024,2432]{1,0:T(8,128)S(1)} %copy-done.15, bf16[1024,608]{0,1:T(8,128)(2,1)S(1)} %fusion.31, bf16[304,2432]{1,0:T(8,128)(2,1)} %collective-permute-done.9, bf16[304,2432]{1,0:T(8,128)(2,1)} %collective-permute-done.8), kind=kOutput, calls=%fused_computation | convolution fusion | flops 3039182848 | bytes 19144704 | tf_op jit(solution)/shard_map/dot_general | solution.py:192
  299.6 15.5 %reduce-scatter.6.cloned.1.call-done = bf16[512,2432]{1,0:T(8,128)(2,1)} async-done(((bf16[1024,2432]{1,0:T(8,128)(2,1)}), bf16[512,2432]{1,0:T(8,128)(2,1)}) %reduce-scatter.6.cloned.1.call-update) | async-done | bytes 2490384 | tf_op jit(solution)/shard_map/reduce_scatter | solution.py:195
  315.1 36.6 %reduce-scatter.8.cloned.1.call-done = bf16[128,2432]{1,0:T(8,128)(2,1)} async-done(((bf16[512,2432]{1,0:T(8,128)(2,1)}), bf16[128,2432]{1,0:T(8,128)(2,1)}) %reduce-scatter.8.cloned.1.call-update) | async-done | bytes 622608 | tf_op jit(solution)/shard_map/reduce_scatter | solution.py:198
  351.8 2.1 fusion.52
  (93 shorter events, 11.6 us)
Async XLA Ops:
  6.5 189.1 %copy-start = (bf16[384,2432]{1,0:T(8,128)(2,1)S(1)}, bf16[384,2432]{1,0:T(8,128)(2,1)}, u32[]{:S(2)}) copy-start(bf16[384,2432]{1,0:T(8,128)(2,1)} %param.23) | copy-start | bytes 5603332
  6.5 8.8 %copy-start.10 = (bf16[20,1,2432]{2,0,1:T(8,128)(2,1)S(1)}, bf16[20,1,2432]{2,0,1:T(8,128)(2,1)}, u32[]{:S(2)}) copy-start(bf16[20,1,2432]{2,0,1:T(8,128)(2,1)} %param.14) | copy-start | bytes 291844
  6.5 40.0 %all-gather.4.cloned.1.call-start = ((), (), s32[]{:S(2)}) async-start(), calls=%async_computation.3 | async-start | bytes 3112960 | tf_op jit(solution)/shard_map/all_gather | solution.py:113
  7.3 223.0 %reduce-scatter.4.cloned.1.call-start = ((), (), s32[]{:S(2)}) async-start(), calls=%async_computation.4 | async-start | bytes 3112960 | tf_op jit(solution)/shard_map/reduce_scatter | solution.py:170
  7.3 70.0 %collective-permute-start.7 = (bf16[2432,608]{0,1:T(8,128)(2,1)}, bf16[2432,608]{0,1:T(8,128)(2,1)}, u32[]{:S(2)}, u32[]{:S(2)}) collective-permute-start(bf16[2432,608]{0,1:T(8,128)(2,1)} %param.24), channel_id=1, source_target_pairs={{0,80},{4,84},{8,88},{12,92},{16,64},{20,68},{24,72},{28,76},{64,1... | collective-permute-start | bytes 8871944 | tf_op jit(solution)/shard_map/ppermute | solution.py:99
  15.3 3.5 copy-start.11
  46.6 2.5 copy-start.2
  56.3 1.4 copy-start.3
  66.7 47.4 %copy-start.4 = (bf16[1088,384]{1,0:T(8,128)(2,1)}, bf16[1088,384]{1,0:T(8,128)(2,1)S(1)}, u32[]{:S(2)}) copy-start(bf16[1088,384]{1,0:T(8,128)(2,1)S(1)} %concatenate.6.refs_0_) | copy-start | bytes 2506756
  66.7 47.3 %collective-permute-start.6 = (bf16[1088,384]{1,0:T(8,128)(2,1)S(1)}, bf16[1088,384]{1,0:T(8,128)(2,1)S(1)}, u32[]{:S(2)}, u32[]{:S(2)}) collective-permute-start(bf16[1088,384]{1,0:T(8,128)(2,1)S(1)} %concatenate.6.refs_0_), channel_id=1, source_target_pairs={{0,28},{4,0},{8,4},{12,8},{16,12},{20,16},{24,20},{28,24},{1,29},{... | collective-permute-start | bytes 2506760 | tf_op jit(solution)/shard_map/ppermute | solution.py:154
  70.1 43.9 %collective-permute-start.5 = (bf16[1088,384]{1,0:T(8,128)(2,1)S(1)}, bf16[1088,384]{1,0:T(8,128)(2,1)S(1)}, u32[]{:S(2)}, u32[]{:S(2)}) collective-permute-start(bf16[1088,384]{1,0:T(8,128)(2,1)S(1)} %concatenate.6.refs_0_), channel_id=1, source_target_pairs={{0,24},{4,28},{8,0},{12,4},{16,8},{20,12},{24,16},{28,20},{1,25},{... | collective-permute-start | bytes 2506760 | tf_op jit(solution)/shard_map/ppermute | solution.py:154
  70.7 43.4 %collective-permute-start.4 = (bf16[1088,384]{1,0:T(8,128)(2,1)S(1)}, bf16[1088,384]{1,0:T(8,128)(2,1)S(1)}, u32[]{:S(2)}, u32[]{:S(2)}) collective-permute-start(bf16[1088,384]{1,0:T(8,128)(2,1)S(1)} %concatenate.6.refs_0_), channel_id=1, source_target_pairs={{0,20},{4,24},{8,28},{12,0},{16,4},{20,8},{24,12},{28,16},{1,21},{... | collective-permute-start | bytes 2506760 | tf_op jit(solution)/shard_map/ppermute | solution.py:154
  74.9 120.8 %collective-permute-start.8 = (bf16[304,2432]{1,0:T(8,128)(2,1)}, bf16[304,2432]{1,0:T(8,128)(2,1)}, u32[]{:S(2)}, u32[]{:S(2)}) collective-permute-start(bf16[304,2432]{1,0:T(8,128)(2,1)} %get-tuple-element.40), channel_id=1, source_target_pairs={{0,80},{4,84},{8,88},{12,92},{16,64},{20,68},{24,72},{28,76},{64,1... | collective-permute-start | bytes 4435976 | tf_op jit(solution)/shard_map/ppermute | solution.py:101
  77.3 41.9 %collective-permute-start.3 = (bf16[1088,384]{1,0:T(8,128)(2,1)S(1)}, bf16[1088,384]{1,0:T(8,128)(2,1)}, u32[]{:S(2)}, u32[]{:S(2)}) collective-permute-start(bf16[1088,384]{1,0:T(8,128)(2,1)S(1)} %concatenate.6.refs_0_), channel_id=1, source_target_pairs={{0,16},{4,20},{8,24},{12,28},{16,0},{20,4},{24,8},{28,12},{1,17},{... | collective-permute-start | bytes 2506760 | tf_op jit(solution)/shard_map/ppermute | solution.py:154
  114.0 57.1 %copy-start.7 = (bf16[1088,384]{1,0:T(8,128)(2,1)}, bf16[1088,384]{1,0:T(8,128)(2,1)S(1)}, u32[]{:S(2)}) copy-start(bf16[1088,384]{1,0:T(8,128)(2,1)S(1)} %collective-permute-done.6.refs_7_) | copy-start | bytes 2506756
  114.0 25.7 %collective-permute-start.2 = (bf16[1088,384]{1,0:T(8,128)(2,1)S(1)}, bf16[1088,384]{1,0:T(8,128)(2,1)}, u32[]{:S(2)}, u32[]{:S(2)}) collective-permute-start(bf16[1088,384]{1,0:T(8,128)(2,1)S(1)} %concatenate.6.refs_0_), channel_id=1, source_target_pairs={{0,12},{4,16},{8,20},{12,24},{16,28},{20,0},{24,4},{28,8},{1,13},{... | collective-permute-start | bytes 2506760 | tf_op jit(solution)/shard_map/ppermute | solution.py:154
  114.0 3.8 %copy-start.8 = (bf16[1088,384]{1,0:T(8,128)(2,1)}, bf16[1088,384]{1,0:T(8,128)(2,1)S(1)}, u32[]{:S(2)}) copy-start(bf16[1088,384]{1,0:T(8,128)(2,1)S(1)} %collective-permute-done.5.refs_6_) | copy-start | bytes 2506756
  114.0 38.0 %collective-permute-start.1 = (bf16[1088,384]{1,0:T(8,128)(2,1)S(1)}, bf16[1088,384]{1,0:T(8,128)(2,1)}, u32[]{:S(2)}, u32[]{:S(2)}) collective-permute-start(bf16[1088,384]{1,0:T(8,128)(2,1)S(1)} %concatenate.6.refs_0_), channel_id=1, source_target_pairs={{0,8},{4,12},{8,16},{12,20},{16,24},{20,28},{24,0},{28,4},{1,9},{5... | collective-permute-start | bytes 2506760 | tf_op jit(solution)/shard_map/ppermute | solution.py:154
  114.1 3.7 %copy-start.9 = (bf16[1088,384]{1,0:T(8,128)(2,1)}, bf16[1088,384]{1,0:T(8,128)(2,1)S(1)}, u32[]{:S(2)}) copy-start(bf16[1088,384]{1,0:T(8,128)(2,1)S(1)} %collective-permute-done.4.refs_5_) | copy-start | bytes 2506756
  114.1 57.0 %collective-permute-start = (bf16[1088,384]{1,0:T(8,128)(2,1)S(1)}, bf16[1088,384]{1,0:T(8,128)(2,1)}, u32[]{:S(2)}, u32[]{:S(2)}) collective-permute-start(bf16[1088,384]{1,0:T(8,128)(2,1)S(1)} %concatenate.6.refs_0_), channel_id=1, source_target_pairs={{0,4},{4,8},{8,12},{12,16},{16,20},{20,24},{24,28},{28,0},{1,5},{5... | collective-permute-start | bytes 2506760 | tf_op jit(solution)/shard_map/ppermute | solution.py:154
  199.6 1.4 copy-start.6
  199.6 35.9 %copy-start.5 = (bf16[8,16,1,2432]{3,1,2,0:T(8,128)(2,1)S(1)}, bf16[8,16,1,2432]{3,1,2,0:T(8,128)(2,1)}, u32[]{:S(2)}) copy-start(bf16[8,16,1,2432]{3,1,2,0:T(8,128)(2,1)} %param.13) | copy-start | bytes 1867780
  199.6 35.9 %copy-start.14 = (f32[2432]{0:T(1024)S(1)}, f32[2432]{0:T(1024)}, u32[]{:S(2)}) copy-start(f32[2432]{0:T(1024)} %get-tuple-element.36) | copy-start | bytes 29188
  199.6 70.8 %all-gather.6.cloned.1.call-start = ((), (), s32[]{:S(2)}) async-start(), calls=%async_computation.7 | async-start | bytes 5603328 | tf_op jit(solution)/shard_map/all_gather | solution.py:186
  201.0 35.1 %copy-start.12 = (f32[2432]{0:T(1024)S(1)}, f32[2432]{0:T(1024)}, u32[]{:S(2)}) copy-start(f32[2432]{0:T(1024)} %get-tuple-element.32) | copy-start | bytes 29188
  201.0 35.1 %copy-start.13 = (f32[2432]{0:T(1024)S(1)}, f32[2432]{0:T(1024)}, u32[]{:S(2)}) copy-start(f32[2432]{0:T(1024)} %get-tuple-element.33) | copy-start | bytes 29188
  201.0 34.5 %collective-permute-start.9 = (bf16[304,2432]{1,0:T(8,128)(2,1)S(1)}, bf16[304,2432]{1,0:T(8,128)(2,1)}, u32[]{:S(2)}, u32[]{:S(2)}) collective-permute-start(bf16[304,2432]{1,0:T(8,128)(2,1)S(1)} %copy-done.6), channel_id=1, source_target_pairs={{0,80},{4,84},{8,88},{12,92},{16,64},{20,68},{24,72},{28,76},{64,1... | collective-permute-start | bytes 4435976 | tf_op jit(solution)/shard_map/ppermute | solution.py:102
  237.4 77.7 %reduce-scatter.6.cloned.1.call-start = ((), (), s32[]{:S(2)}) async-start(), calls=%async_computation.5 | async-start | bytes 7471104 | tf_op jit(solution)/shard_map/reduce_scatter | solution.py:195
  284.2 7.3 %copy-start.15 = (f32[1024,2432]{1,0:T(8,128)S(1)}, f32[1024,2432]{1,0:T(8,128)}, u32[]{:S(2)}) copy-start(f32[1024,2432]{1,0:T(8,128)} %fusion.61) | copy-start | bytes 29884420
  299.6 54.3 %copy-start.1 = (bf16[384,2432]{1,0:T(8,128)(2,1)S(1)}, bf16[384,2432]{1,0:T(8,128)(2,1)}, u32[]{:S(2)}) copy-start(bf16[384,2432]{1,0:T(8,128)(2,1)} %param.23) | copy-start | bytes 5603332
  299.6 52.2 %reduce-scatter.8.cloned.1.call-start = ((), (), s32[]{:S(2)}) async-start(), calls=%async_computation.6 | async-start | bytes 3112960 | tf_op jit(solution)/shard_map/reduce_scatter | solution.py:198
Sparse Core Ops, SparseCore 0:
  9.0 37.5 all-gather.3
  199.7 30.4 reduce-scatter.3
  237.5 32.7 all-gather.5
  299.7 15.3 reduce-scatter.5
  317.5 34.2 reduce-scatter.7
